TPU v7x, 32 devices: a whole 2x2x4 slice. The times are simulated.
32 devices in a mesh: parts: 2 (over x), ref: 16 (over z, y, core).
Axes of the slice: x: 2, y: 2, z: 4, core: 2. Of those that a mesh axis runs over, the one named last changes fastest.
Arguments:
- queries: float32 [4096, 128], P('parts'), parts along dimension 0, may hold values from -15 to 15, as said below
- references: float32 [65536, 128], P(('parts', 'ref')), parts along dimension 0, may hold values from -15 to 15
- query_ids: int32 [4096], P('parts'), parts along dimension 0, may hold values from 0 to 32767, as said below
- spread: float32 [128], replicated, may hold values from 0.5 to 2
- cotangent: float32 [4096], P('parts'), parts along dimension 0, may hold values from -4 to 4
Outputs:
- query_grad: float32 [4096, 128], P(('parts', 'ref')), parts along dimension 0
- reference_grad: float32 [65536, 128], P(('parts', 'ref')), parts along dimension 0
- spread_grad: float32 [256], P('parts'), parts along dimension 0
There are 2 independent parts, one for each index of `parts`. A program takes and returns all parts, laid end to end along the dimension named above; an argument that names none is the same for every part. Nothing has to cross between parts.
Inputs may be any that keep to these rules, and one draw needn't show every extreme that they name: `query_ids`: distinct rows of the references; query i is the reference row query_ids_i. `queries`: row i equals row query_ids_i of references.
All inputs are finite; a program needn't handle non-finite values.
Results may differ from a plain program's by a relative error of at most 0.014.
Values sent between devices are 32-bit elements; how exact they have to be, the bound alone decides.
No kernel may reach another device: no remote copies, remote signals or barrier semaphores. Data moves between devices by JAX's collectives and lax.ppermute only.
A program may use at most 64 MiB of HBM per device.

v0:
```python
import jax
import jax.numpy as jnp
from jax import lax
from jax.sharding import PartitionSpec as P


def block_score(query_block, id_block, references, rnorm, inv, ref_start):
    cross = lax.dot_general(
        query_block * inv,
        references,
        (((1,), (1,)), ((), ())),
        precision=lax.Precision.HIGHEST,
        preferred_element_type=jnp.float32,
    )
    qnorm = jnp.sum(query_block * query_block * inv, axis=1)
    score = cross - 0.5 * qnorm[:, None] - 0.5 * rnorm[None, :]
    local_ids = id_block - ref_start
    self_mask = local_ids[:, None] == lax.iota(jnp.int32, references.shape[0])[None, :]
    return (jnp.where(self_mask, -jnp.inf, score), self_mask)


def on_device(queries, references, query_ids, spread, cotangent):
    n_query = queries.shape[0]
    n_feat = queries.shape[1]
    n_ref = references.shape[0]
    block_rows = min(512, n_query)
    n_blocks = n_query // block_rows
    inv = 1.0 / (spread * spread)
    rnorm = jnp.sum(references * references * inv, axis=1)
    ref_start = lax.axis_index("ref") * n_ref
    query_blocks = queries.reshape(n_blocks, block_rows, n_feat)
    id_blocks = query_ids.reshape(n_blocks, block_rows)
    weight_blocks = cotangent.reshape(n_blocks, block_rows)

    def local_density(items):
        query_block, id_block = items
        score, self_mask = block_score(query_block, id_block, references, rnorm, inv, ref_start)
        local_peak = jnp.max(score, axis=1)
        local_total = jnp.sum(jnp.exp(score - local_peak[:, None]), axis=1)
        return (local_peak, local_total)

    local_peak, local_total = lax.map(local_density, (query_blocks, id_blocks))
    local_peak = local_peak.reshape(n_query)
    local_total = local_total.reshape(n_query)
    peak = lax.pmax(local_peak, "ref")
    total = lax.psum(local_total * jnp.exp(local_peak - peak), "ref")
    ref_low = references.astype(jnp.bfloat16)
    query_low_blocks = query_blocks.astype(jnp.bfloat16)

    def backward(carry, items):
        pushed, column = carry
        query_block, query_low, id_block, cot_block, peak_block, total_block = items
        score, self_mask = block_score(query_block, id_block, references, rnorm, inv, ref_start)
        weight = jnp.where(
            self_mask,
            0.0,
            cot_block[:, None] * jnp.exp(score - peak_block[:, None]) / total_block[:, None],
        ).astype(jnp.bfloat16)
        pulled = jnp.dot(weight, ref_low, preferred_element_type=jnp.float32)
        pushed = pushed + lax.dot_general(
            weight, query_low, (((0,), (0,)), ((), ())), preferred_element_type=jnp.float32
        )
        column = column + jnp.sum(weight.astype(jnp.float32), axis=0)
        return ((pushed, column), pulled)

    init = (jnp.zeros((n_ref, n_feat), jnp.float32), jnp.zeros((n_ref,), jnp.float32))
    items = (
        query_blocks,
        query_low_blocks,
        id_blocks,
        weight_blocks,
        peak.reshape(n_blocks, block_rows),
        total.reshape(n_blocks, block_rows),
    )
    (pushed, column), pulled = lax.scan(backward, init, items)
    pulled = pulled.reshape(n_query, n_feat)
    reference_grad = (pushed - references * column[:, None]) * inv
    ref_terms = jnp.sum(references * reference_grad, axis=0)
    weight_total = jnp.sum(cotangent)
    own_rows = n_query // lax.axis_size("ref")
    own_start = lax.axis_index("ref") * own_rows
    summed_pull, summed_terms = lax.psum((pulled, ref_terms), "ref")
    every_grad = (summed_pull - queries * cotangent[:, None]) * inv
    summed = jnp.sum(queries * every_grad, axis=0) + summed_terms
    query_grad = lax.dynamic_slice_in_dim(every_grad, own_start, own_rows, 0)
    spread_grad = -summed / spread - weight_total / spread
    return (query_grad, reference_grad, spread_grad)


def solution(mesh):
    placed = (P("parts", None), P(("parts", "ref"), None), P("parts"), P(), P("parts"))
    return jax.shard_map(
        on_device,
        mesh=mesh,
        in_specs=placed,
        out_specs=(P(("parts", "ref"), None), P(("parts", "ref"), None), P("parts")),
        check_vma=False,
    )
```

profile of v0, /device:TPU:0, one launch (start us, length us, event | category | flops | bytes accessed | tf_op | source)
XLA Modules:
  0.0 282.6 jit_solution(32626793319487471)
XLA Ops:
  9.3 1.3 convert_element_type.12
  10.6 1.9 fusion.15
  12.5 30.2 %while.27 = (s32[]{:T(128)}, f32[4,512]{1,0:T(4,128)S(1)}, f32[4,512]{1,0:T(4,128)S(1)}, s32[4,512]{1,0:T(4,128)S(1)}, s32[]{:T(128)}, /*index=5*/f32[4,512,128]...) while((s32[]{:T(128)}, f32[4,512]{1,0:T(4,128)S(1)}, ...), condition=%wide.region_5.6_spmd, body=%wide.region_1.5_spmd.sunk | while | flops 1618216448 | bytes 10015885 | solution.py:42
  12.6 1.1 fusion.32
  13.7 5.6 %fusion.33 = (f32[512]{0:T(512)S(1)}, f32[512,2048]{1,0:T(8,128)S(1)}) fusion(f32[2048]{0:T(1024)S(1)} %broadcast_multiply_fusion.8, f32[512]{0:T(512)S(1)} %broadcast_multiply_fusion.9, f32[2048,128]{1,0:T(8,128)} %get-tuple-element.432, f32[4,512,128]{2,1,0:T(8,128)} %get-tuple-element.430, s32[]{:T(128)S(6)} %copy.16, ...), kind=kOutput, calls=%fused_computation.45.clone.1 | convolution fusion | flops 1615920640 | bytes 5519876 | tf_op jit(solution)/shard_map/while/body/eval_jaxpr/dot_general | solution.py:8
  20.1 1.1 fusion.32
  21.2 5.6 %fusion.33 = (f32[512]{0:T(512)S(1)}, f32[512,2048]{1,0:T(8,128)S(1)}) fusion(f32[2048]{0:T(1024)S(1)} %broadcast_multiply_fusion.8, f32[512]{0:T(512)S(1)} %broadcast_multiply_fusion.9, f32[2048,128]{1,0:T(8,128)} %get-tuple-element.432, f32[4,512,128]{2,1,0:T(8,128)} %get-tuple-element.430, s32[]{:T(128)S(6)} %copy.16, ...), kind=kOutput, calls=%fused_computation.45.clone.1 | convolution fusion | flops 1615920640 | bytes 5519876 | tf_op jit(solution)/shard_map/while/body/eval_jaxpr/dot_general | solution.py:8
  27.7 1.1 fusion.32
  28.8 5.6 %fusion.33 = (f32[512]{0:T(512)S(1)}, f32[512,2048]{1,0:T(8,128)S(1)}) fusion(f32[2048]{0:T(1024)S(1)} %broadcast_multiply_fusion.8, f32[512]{0:T(512)S(1)} %broadcast_multiply_fusion.9, f32[2048,128]{1,0:T(8,128)} %get-tuple-element.432, f32[4,512,128]{2,1,0:T(8,128)} %get-tuple-element.430, s32[]{:T(128)S(6)} %copy.16, ...), kind=kOutput, calls=%fused_computation.45.clone.1 | convolution fusion | flops 1615920640 | bytes 5519876 | tf_op jit(solution)/shard_map/while/body/eval_jaxpr/dot_general | solution.py:8
  35.2 1.1 fusion.32
  36.3 5.6 %fusion.33 = (f32[512]{0:T(512)S(1)}, f32[512,2048]{1,0:T(8,128)S(1)}) fusion(f32[2048]{0:T(1024)S(1)} %broadcast_multiply_fusion.8, f32[512]{0:T(512)S(1)} %broadcast_multiply_fusion.9, f32[2048,128]{1,0:T(8,128)} %get-tuple-element.432, f32[4,512,128]{2,1,0:T(8,128)} %get-tuple-element.430, s32[]{:T(128)S(6)} %copy.16, ...), kind=kOutput, calls=%fused_computation.45.clone.1 | convolution fusion | flops 1615920640 | bytes 5519876 | tf_op jit(solution)/shard_map/while/body/eval_jaxpr/dot_general | solution.py:8
  42.8 35.5 %pmax.7 = f32[2048]{0:T(1024)S(1)} all-reduce(f32[2048]{0:T(1024)S(1)} %bitcast.87), channel_id=1, replica_groups=mesh['parts'=2,'ref'=16] {'ref'}, use_global_device_ids=true, to_apply=%region_6.7 | all-reduce | flops 2048 | bytes 16384 | tf_op jit(solution)/shard_map/pmax | solution.py:45
  78.3 30.2 %psum.21 = f32[4,512]{1,0:T(4,128)S(1)} all-reduce(f32[4,512]{1,0:T(4,128)S(1)} %reshape.78), channel_id=1, replica_groups=mesh['parts'=2,'ref'=16] {'ref'}, use_global_device_ids=true, to_apply=%region_7.8 | all-reduce | flops 2048 | bytes 16384 | tf_op jit(solution)/shard_map/psum | solution.py:46
  108.5 40.9 %while.28 = (s32[]{:T(128)}, f32[2048,128]{1,0:T(8,128)S(1)}, f32[2048]{0:T(1024)S(1)}, f32[4,512,128]{2,1,0:T(8,128)}, s32[4,512]{1,0:T(4,128)S(1)}, /*index=5*...) while((s32[]{:T(128)}, f32[2048,128]{1,0:T(8,128)S(1)}, ...), condition=%wide.region_11.12_spmd.clone, body=%wide.region_8.11_spmd.clone.sunk | while | flops 2159809024 | bytes 10970320 | solution.py:75
  109.7 6.4 %convert_reduce_fusion.2 = (f32[2048]{0:T(1024)S(1)}, bf16[512,2048]{1,0:T(8,128)(2,1)S(1)}) fusion(f32[512]{0:T(512)S(1)} %bitcast.89, f32[512]{0:T(512)S(1)} %bitcast.90, f32[2048]{0:T(1024)S(1)} %broadcast_multiply_fusion.10, f32[512]{0:T(512)S(1)} %broadcast_multiply_fusion.11, f32[2048,128]{1,0:T(8,128)} %get-tuple-element.479, ...), kind=kOutput, calls=%fused_computation.13.clone.1 | convolution fusion | flops 1622210560 | bytes 3435012 | tf_op jit(solution)/shard_map/while/body/eval_jaxpr/dot_general | solution.py:8
  116.1 1.2 convolution_add_fusion.2
  117.3 1.4 fusion.40
  119.9 6.4 %convert_reduce_fusion.2 = (f32[2048]{0:T(1024)S(1)}, bf16[512,2048]{1,0:T(8,128)(2,1)S(1)}) fusion(f32[512]{0:T(512)S(1)} %bitcast.89, f32[512]{0:T(512)S(1)} %bitcast.90, f32[2048]{0:T(1024)S(1)} %broadcast_multiply_fusion.10, f32[512]{0:T(512)S(1)} %broadcast_multiply_fusion.11, f32[2048,128]{1,0:T(8,128)} %get-tuple-element.479, ...), kind=kOutput, calls=%fused_computation.13.clone.1 | convolution fusion | flops 1622210560 | bytes 3435012 | tf_op jit(solution)/shard_map/while/body/eval_jaxpr/dot_general | solution.py:8
  126.3 1.2 convolution_add_fusion.2
  127.5 1.4 fusion.40
  128.9 1.1 fusion.39
  130.1 6.4 %convert_reduce_fusion.2 = (f32[2048]{0:T(1024)S(1)}, bf16[512,2048]{1,0:T(8,128)(2,1)S(1)}) fusion(f32[512]{0:T(512)S(1)} %bitcast.89, f32[512]{0:T(512)S(1)} %bitcast.90, f32[2048]{0:T(1024)S(1)} %broadcast_multiply_fusion.10, f32[512]{0:T(512)S(1)} %broadcast_multiply_fusion.11, f32[2048,128]{1,0:T(8,128)} %get-tuple-element.479, ...), kind=kOutput, calls=%fused_computation.13.clone.1 | convolution fusion | flops 1622210560 | bytes 3435012 | tf_op jit(solution)/shard_map/while/body/eval_jaxpr/dot_general | solution.py:8
  136.5 1.2 convolution_add_fusion.2
  137.7 1.4 fusion.40
  139.1 1.1 fusion.39
  140.3 6.4 %convert_reduce_fusion.2 = (f32[2048]{0:T(1024)S(1)}, bf16[512,2048]{1,0:T(8,128)(2,1)S(1)}) fusion(f32[512]{0:T(512)S(1)} %bitcast.89, f32[512]{0:T(512)S(1)} %bitcast.90, f32[2048]{0:T(1024)S(1)} %broadcast_multiply_fusion.10, f32[512]{0:T(512)S(1)} %broadcast_multiply_fusion.11, f32[2048,128]{1,0:T(8,128)} %get-tuple-element.479, ...), kind=kOutput, calls=%fused_computation.13.clone.1 | convolution fusion | flops 1622210560 | bytes 3435012 | tf_op jit(solution)/shard_map/while/body/eval_jaxpr/dot_general | solution.py:8
  146.7 1.2 convolution_add_fusion.2
  147.9 1.4 fusion.40
  150.0 90.4 %all-reduce.2.cloned.1.call-done = f32[2048,128]{1,0:T(8,128)} async-done(((f32[2048,128]{1,0:T(8,128)}), f32[2048,128]{1,0:T(8,128)}) %all-reduce.2.cloned.1.call-update) | async-done | bytes 1048592 | tf_op jit(solution)/shard_map/psum | solution.py:82
  240.5 3.0 %multiply_reduce_fusion = (f32[128]{0:T(128)S(1)}, f32[2048,128]{1,0:T(8,128)}, f32[128]{0:T(128)S(1)}, f32[2048,128]{1,0:T(8,128)S(1)}) fusion(f32[2048,128]{1,0:T(8,128)} %get-tuple-element.491, f32[128]{0:T(128)S(1)} %get-tuple-element.498, f32[2048,128]{1,0:T(8,128)S(1)} %get-tuple-element.133, f32[2048]{0:T(1024)S(1)} %get-tuple-element.134, ...), kind=kLoop, calls=%fused_computation.36 | loop fusion | flops 2621184 | bytes 6309376 | tf_op jit(solution)/shard_map/reduce_sum | solution.py:78
  243.5 30.4 %psum.23 = f32[128]{0:T(128)S(1)} all-reduce(f32[128]{0:T(128)S(1)} %get-tuple-element.231), channel_id=1, replica_groups=mesh['parts'=2,'ref'=16] {'ref'}, use_global_device_ids=true, to_apply=%region_15.16 | all-reduce | flops 128 | bytes 1024 | tf_op jit(solution)/shard_map/psum | solution.py:82
  274.5 1.2 divide_subtract_fusion
  (71 shorter events, 9.2 us)
Async XLA Ops:
  7.2 233.3 %all-reduce.2.cloned.1.call-start = ((), (), s32[]{:S(2)}) async-start(), calls=%async_computation | async-start | bytes 2097152 | tf_op jit(solution)/shard_map/psum | solution.py:82
  108.5 40.9 %copy-start = (f32[2048]{0:T(1024)S(1)}, f32[2048]{0:T(1024)}, u32[]{:S(2)}) copy-start(f32[2048]{0:T(1024)} %param.13) | copy-start | bytes 24580
  149.3 125.2 %copy-start.1 = (f32[128]{0:T(128)S(1)}, f32[128]{0:T(128)}, u32[]{:S(2)}) copy-start(f32[128]{0:T(128)} %param.12) | copy-start | bytes 1540
Sparse Core Ops, SparseCore 0:
  149.5 90.9 all-reduce.1
where the time goes:
time: 283 us
  blocking collectives  96.1 us (34%)
  waiting for transfers between devices  90.5 us (32%)
  matrix products  58.4 us (21%)
  other arithmetic  20.5 us (7%)
  between operations  14.2 us (5%)
    psum x1, waiting for transfers between devices, on_device(): summed_pull, summed_terms = lax.psum((pulled, ref_terms), 'ref')  90.4 us
    dot_general x8, matrix products, block_score(): lax.dot_general(query_block * inv, references, (((1,), (1,)), ((), ())),...  47.9 us
    pmax x1, blocking collectives, on_device(): peak = lax.pmax(local_peak, 'ref')  35.5 us
    psum x1, blocking collectives, on_device(): summed_pull, summed_terms = lax.psum((pulled, ref_terms), 'ref')  30.4 us
    psum x1, blocking collectives, on_device(): total = lax.psum(local_total * jnp.exp(local_peak - peak), 'ref')  30.2 us
    reduce_sum x8, other arithmetic, block_score(): qnorm = jnp.sum(query_block * query_block * inv, axis=1)  8.81 us
    dot_general x4, matrix products, backward(): pulled = jnp.dot(weight, ref_low, preferred_element_type=jnp.float32)  5.7 us
  transfers between devices with their start and end apart: 1, of which 1 were waited for; matrix products, arithmetic and copies ran while one was open for 0% of the time, Pallas kernels for 0%

commit v1 on v0

--- a/solution.py
+++ b/solution.py
@@ -43,7 +43,7 @@
     local_peak = local_peak.reshape(n_query)
     local_total = local_total.reshape(n_query)
     peak = lax.pmax(local_peak, "ref")
-    total = lax.psum(local_total * jnp.exp(local_peak - peak), "ref")
+    total = jnp.sum(lax.all_gather(local_total * jnp.exp(local_peak - peak), "ref"), axis=0)
     ref_low = references.astype(jnp.bfloat16)
     query_low_blocks = query_blocks.astype(jnp.bfloat16)
 

time: 283 us -> 272 us (0.961)
  blocking collectives: 96.1 us -> 83.5 us
    psum x1 -> x0, blocking collectives: 30.2 us -> none  [on_device(): total = lax.psum(local_total * jnp.exp(local_peak - peak), 'ref')]
    all_gather x0 -> x1, blocking collectives: none -> 17.7 us  [on_device(): lax.all_gather(local_total * jnp.exp(local_peak - peak), 'ref')]
where the time goes in v1:
time: 272 us
  waiting for transfers between devices  91.9 us (34%)
  blocking collectives  83.5 us (31%)
  matrix products  58.4 us (21%)
  other arithmetic  20.6 us (8%)
  between operations  14.2 us (5%)
    psum x1, waiting for transfers between devices, on_device(): summed_pull, summed_terms = lax.psum((pulled, ref_terms), 'ref')  91.9 us
    dot_general x8, matrix products, block_score(): lax.dot_general(query_block * inv, references, (((1,), (1,)), ((), ())),...  47.9 us
    pmax x1, blocking collectives, on_device(): peak = lax.pmax(local_peak, 'ref')  35.5 us
    psum x1, blocking collectives, on_device(): summed_pull, summed_terms = lax.psum((pulled, ref_terms), 'ref')  30.4 us
    all_gather x1, blocking collectives, on_device(): lax.all_gather(local_total * jnp.exp(local_peak - peak), 'ref')  17.7 us
    reduce_sum x8, other arithmetic, block_score(): qnorm = jnp.sum(query_block * query_block * inv, axis=1)  8.81 us
    dot_general x4, matrix products, backward(): pulled = jnp.dot(weight, ref_low, preferred_element_type=jnp.float32)  5.7 us
  transfers between devices with their start and end apart: 1, of which 1 were waited for; matrix products, arithmetic and copies ran while one was open for 0% of the time, Pallas kernels for 0%

profile of v1, /device:TPU:0, one launch (start us, length us, event | category | flops | bytes accessed | tf_op | source)
XLA Modules:
  0.0 271.6 jit_solution(3731734360498518854)
XLA Ops:
  9.3 1.3 convert_element_type.12
  10.6 1.9 fusion.15
  12.5 30.2 %while.27 = (s32[]{:T(128)}, f32[4,512]{1,0:T(4,128)S(1)}, f32[4,512]{1,0:T(4,128)S(1)}, s32[4,512]{1,0:T(4,128)S(1)}, s32[]{:T(128)}, /*index=5*/f32[4,512,128]...) while((s32[]{:T(128)}, f32[4,512]{1,0:T(4,128)S(1)}, ...), condition=%wide.region_5.6_spmd, body=%wide.region_1.5_spmd.sunk | while | flops 1618216448 | bytes 10015885 | solution.py:42
  12.6 1.1 fusion.32
  13.7 5.6 %fusion.33 = (f32[512]{0:T(512)S(1)}, f32[512,2048]{1,0:T(8,128)S(1)}) fusion(f32[2048]{0:T(1024)S(1)} %broadcast_multiply_fusion.8, f32[512]{0:T(512)S(1)} %broadcast_multiply_fusion.9, f32[2048,128]{1,0:T(8,128)} %get-tuple-element.432, f32[4,512,128]{2,1,0:T(8,128)} %get-tuple-element.430, s32[]{:T(128)S(6)} %copy.16, ...), kind=kOutput, calls=%fused_computation.45.clone.1 | convolution fusion | flops 1615920640 | bytes 5519876 | tf_op jit(solution)/shard_map/while/body/eval_jaxpr/dot_general | solution.py:8
  20.1 1.1 fusion.32
  21.2 5.6 %fusion.33 = (f32[512]{0:T(512)S(1)}, f32[512,2048]{1,0:T(8,128)S(1)}) fusion(f32[2048]{0:T(1024)S(1)} %broadcast_multiply_fusion.8, f32[512]{0:T(512)S(1)} %broadcast_multiply_fusion.9, f32[2048,128]{1,0:T(8,128)} %get-tuple-element.432, f32[4,512,128]{2,1,0:T(8,128)} %get-tuple-element.430, s32[]{:T(128)S(6)} %copy.16, ...), kind=kOutput, calls=%fused_computation.45.clone.1 | convolution fusion | flops 1615920640 | bytes 5519876 | tf_op jit(solution)/shard_map/while/body/eval_jaxpr/dot_general | solution.py:8
  27.7 1.1 fusion.32
  28.8 5.6 %fusion.33 = (f32[512]{0:T(512)S(1)}, f32[512,2048]{1,0:T(8,128)S(1)}) fusion(f32[2048]{0:T(1024)S(1)} %broadcast_multiply_fusion.8, f32[512]{0:T(512)S(1)} %broadcast_multiply_fusion.9, f32[2048,128]{1,0:T(8,128)} %get-tuple-element.432, f32[4,512,128]{2,1,0:T(8,128)} %get-tuple-element.430, s32[]{:T(128)S(6)} %copy.16, ...), kind=kOutput, calls=%fused_computation.45.clone.1 | convolution fusion | flops 1615920640 | bytes 5519876 | tf_op jit(solution)/shard_map/while/body/eval_jaxpr/dot_general | solution.py:8
  36.3 5.6 %fusion.33 = (f32[512]{0:T(512)S(1)}, f32[512,2048]{1,0:T(8,128)S(1)}) fusion(f32[2048]{0:T(1024)S(1)} %broadcast_multiply_fusion.8, f32[512]{0:T(512)S(1)} %broadcast_multiply_fusion.9, f32[2048,128]{1,0:T(8,128)} %get-tuple-element.432, f32[4,512,128]{2,1,0:T(8,128)} %get-tuple-element.430, s32[]{:T(128)S(6)} %copy.16, ...), kind=kOutput, calls=%fused_computation.45.clone.1 | convolution fusion | flops 1615920640 | bytes 5519876 | tf_op jit(solution)/shard_map/while/body/eval_jaxpr/dot_general | solution.py:8
  42.8 35.5 %pmax.7 = f32[2048]{0:T(1024)S(1)} all-reduce(f32[2048]{0:T(1024)S(1)} %bitcast.87), channel_id=1, replica_groups=mesh['parts'=2,'ref'=16] {'ref'}, use_global_device_ids=true, to_apply=%region_6.7 | all-reduce | flops 2048 | bytes 16384 | tf_op jit(solution)/shard_map/pmax | solution.py:45
  78.3 17.7 %all-gather = f32[32768]{0:T(1024)S(1)} all-gather(f32[2048]{0:T(1024)S(1)} %exponential_multiply_fusion), channel_id=2, replica_groups=mesh['parts'=2,'ref'=16] {'ref'}, dimensions={0}, use_global_device_ids=true | all-gather | bytes 139264 | tf_op jit(solution)/shard_map/all_gather | solution.py:46
  96.0 40.8 %while.28 = (s32[]{:T(128)}, f32[2048,128]{1,0:T(8,128)S(1)}, f32[2048]{0:T(1024)S(1)}, f32[4,512,128]{2,1,0:T(8,128)}, s32[4,512]{1,0:T(4,128)S(1)}, /*index=5*...) while((s32[]{:T(128)}, f32[2048,128]{1,0:T(8,128)S(1)}, ...), condition=%wide.region_11.12_spmd.clone, body=%wide.region_8.11_spmd.clone.sunk | while | flops 2159809024 | bytes 10970320 | solution.py:75
  96.1 1.1 fusion.39
  97.2 6.4 %convert_reduce_fusion.2 = (f32[2048]{0:T(1024)S(1)}, bf16[512,2048]{1,0:T(8,128)(2,1)S(1)}) fusion(f32[512]{0:T(512)S(1)} %bitcast.89, f32[512]{0:T(512)S(1)} %bitcast.90, f32[2048]{0:T(1024)S(1)} %broadcast_multiply_fusion.10, f32[512]{0:T(512)S(1)} %broadcast_multiply_fusion.11, f32[2048,128]{1,0:T(8,128)} %get-tuple-element.479, ...), kind=kOutput, calls=%fused_computation.13.clone.1 | convolution fusion | flops 1622210560 | bytes 3435012 | tf_op jit(solution)/shard_map/while/body/eval_jaxpr/dot_general | solution.py:8
  103.6 1.2 convolution_add_fusion.2
  104.8 1.4 fusion.40
  107.4 6.4 %convert_reduce_fusion.2 = (f32[2048]{0:T(1024)S(1)}, bf16[512,2048]{1,0:T(8,128)(2,1)S(1)}) fusion(f32[512]{0:T(512)S(1)} %bitcast.89, f32[512]{0:T(512)S(1)} %bitcast.90, f32[2048]{0:T(1024)S(1)} %broadcast_multiply_fusion.10, f32[512]{0:T(512)S(1)} %broadcast_multiply_fusion.11, f32[2048,128]{1,0:T(8,128)} %get-tuple-element.479, ...), kind=kOutput, calls=%fused_computation.13.clone.1 | convolution fusion | flops 1622210560 | bytes 3435012 | tf_op jit(solution)/shard_map/while/body/eval_jaxpr/dot_general | solution.py:8
  113.8 1.2 convolution_add_fusion.2
  115.0 1.4 fusion.40
  116.5 1.1 fusion.39
  117.6 6.4 %convert_reduce_fusion.2 = (f32[2048]{0:T(1024)S(1)}, bf16[512,2048]{1,0:T(8,128)(2,1)S(1)}) fusion(f32[512]{0:T(512)S(1)} %bitcast.89, f32[512]{0:T(512)S(1)} %bitcast.90, f32[2048]{0:T(1024)S(1)} %broadcast_multiply_fusion.10, f32[512]{0:T(512)S(1)} %broadcast_multiply_fusion.11, f32[2048,128]{1,0:T(8,128)} %get-tuple-element.479, ...), kind=kOutput, calls=%fused_computation.13.clone.1 | convolution fusion | flops 1622210560 | bytes 3435012 | tf_op jit(solution)/shard_map/while/body/eval_jaxpr/dot_general | solution.py:8
  124.0 1.2 convolution_add_fusion.2
  125.2 1.4 fusion.40
  126.7 1.1 fusion.39
  127.8 6.4 %convert_reduce_fusion.2 = (f32[2048]{0:T(1024)S(1)}, bf16[512,2048]{1,0:T(8,128)(2,1)S(1)}) fusion(f32[512]{0:T(512)S(1)} %bitcast.89, f32[512]{0:T(512)S(1)} %bitcast.90, f32[2048]{0:T(1024)S(1)} %broadcast_multiply_fusion.10, f32[512]{0:T(512)S(1)} %broadcast_multiply_fusion.11, f32[2048,128]{1,0:T(8,128)} %get-tuple-element.479, ...), kind=kOutput, calls=%fused_computation.13.clone.1 | convolution fusion | flops 1622210560 | bytes 3435012 | tf_op jit(solution)/shard_map/while/body/eval_jaxpr/dot_general | solution.py:8
  134.2 1.2 convolution_add_fusion.2
  135.4 1.4 fusion.40
  137.6 91.9 %all-reduce.2.cloned.1.call-done = f32[2048,128]{1,0:T(8,128)} async-done(((f32[2048,128]{1,0:T(8,128)}), f32[2048,128]{1,0:T(8,128)}) %all-reduce.2.cloned.1.call-update) | async-done | bytes 1048592 | tf_op jit(solution)/shard_map/psum | solution.py:82
  229.5 3.0 %multiply_reduce_fusion = (f32[128]{0:T(128)S(1)}, f32[2048,128]{1,0:T(8,128)}, f32[128]{0:T(128)S(1)}, f32[2048,128]{1,0:T(8,128)S(1)}) fusion(f32[2048,128]{1,0:T(8,128)} %get-tuple-element.491, f32[128]{0:T(128)S(1)} %get-tuple-element.498, f32[2048,128]{1,0:T(8,128)S(1)} %get-tuple-element.133, f32[2048]{0:T(1024)S(1)} %get-tuple-element.134, ...), kind=kLoop, calls=%fused_computation.36 | loop fusion | flops 2621184 | bytes 6309376 | tf_op jit(solution)/shard_map/reduce_sum | solution.py:78
  232.4 30.4 %psum.15 = f32[128]{0:T(128)S(1)} all-reduce(f32[128]{0:T(128)S(1)} %get-tuple-element.231), channel_id=1, replica_groups=mesh['parts'=2,'ref'=16] {'ref'}, use_global_device_ids=true, to_apply=%region_15.16 | all-reduce | flops 128 | bytes 1024 | tf_op jit(solution)/shard_map/psum | solution.py:82
  263.5 1.2 divide_subtract_fusion
  (73 shorter events, 9.2 us)
Async XLA Ops:
  7.2 222.3 %all-reduce.2.cloned.1.call-start = ((), (), s32[]{:S(2)}) async-start(), calls=%async_computation | async-start | bytes 2097152 | tf_op jit(solution)/shard_map/psum | solution.py:82
  96.0 40.9 %copy-start = (f32[2048]{0:T(1024)S(1)}, f32[2048]{0:T(1024)}, u32[]{:S(2)}) copy-start(f32[2048]{0:T(1024)} %param.13) | copy-start | bytes 24580
  136.8 126.6 %copy-start.1 = (f32[128]{0:T(128)S(1)}, f32[128]{0:T(128)}, u32[]{:S(2)}) copy-start(f32[128]{0:T(128)} %param.12) | copy-start | bytes 1540
Sparse Core Ops, SparseCore 0:
  137.0 92.4 all-reduce.1
